TPU v7x, 256 devices: a whole 4x4x8 slice. The times are simulated.
256 devices in a mesh: gx: 8 (over x, core), yz: 32 (over z, y).
Axes of the slice: x: 4, y: 4, z: 8, core: 2. Of those that a mesh axis runs over, the one named last changes fastest.
Arguments:
- velocity: float32 [3, 256, 512, 128], P(None, 'gx', 'yz'), may hold values from -6 to 6
- old_pressure: float32 [256, 512, 128], P('gx', 'yz'), may hold values from -3 to 3
- delta_weight: bfloat16 [8, 1024, 128, 128], P('gx', 'yz'), may hold values from -0.5 to 0.5
- marker_target: float32 [8, 1024, 3, 128], P('gx', 'yz'), may hold values from -6 to 6
- pair_owner: int32 [8, 1024, 1], P('gx', 'yz'), may hold values from 0 to 31; in each aligned block of 32 rows (0 to 31, 32 to 63, ..., all dimensions but the last counted through in order) at most 4 rows name the same one
- pair_grain: int32 [8, 1024], P('gx', 'yz'), may hold values from 0 to 31
- box_anchor: int32 [8, 1024, 3], P('gx', 'yz'), may hold values from 0 to 120, as said below
Outputs:
- new_velocity: float32 [3, 256, 512, 128], P(None, 'gx', 'yz')
- pressure: float32 [256, 512, 128], P('gx', 'yz')
Inputs may be any that keep to these rules, and one draw needn't show every extreme that they name: Block r of slab i lies on tile r // 32 of that slab; its grain is owned by tile pair_owner of the same slab. Among the 32 blocks of one tile at most 4 name the same owner, and some tile reaches 4. `pair_grain`: blocks of one slab with equal owner and grain slot belong to one grain. `box_anchor`: column 0 is at most 28, column 1 at most 12, column 2 at most 120, and each of these is reached, so every box lies inside its tile.
All inputs are finite; a program needn't handle non-finite values.
Results may differ from a plain program's by a relative error of at most 0.002.
Values may be sent and summed in bfloat16 or wider, within the bound.
No kernel may reach another device: no remote copies, remote signals or barrier semaphores. Data moves between devices by JAX's collectives and lax.ppermute only.
A program may use at most 128 MiB of HBM per device.

v0:
```python
import jax
import jax.numpy as jnp
from jax import lax
from jax.sharding import PartitionSpec as P

BX = 4
BZ = 4
BY = 8
step_size = 0.1
viscosity = 1.5


def extended(block, sides, width):
    for axis, dim in sides:
        count = lax.axis_size(axis)
        forward = [(i, i + 1) for i in range(count - 1)]
        forward.append((count - 1, 0))
        backward = [(target, source) for source, target in forward]
        low = lax.ppermute(
            lax.slice_in_dim(block, block.shape[dim] - width, None, axis=dim), axis, forward
        )
        high = lax.ppermute(lax.slice_in_dim(block, 0, width, axis=dim), axis, backward)
        block = jnp.concatenate([low, block, high], axis=dim)
    return block


def inner(padded):
    return padded[..., 1:-1, 1:-1, :]


def along_x(padded):
    return 0.5 * (padded[..., 2:, 1:-1, :] - padded[..., :-2, 1:-1, :])


def along_z(padded):
    return 0.5 * (padded[..., 1:-1, 2:, :] - padded[..., 1:-1, :-2, :])


def along_y(field):
    return 0.5 * (jnp.roll(field, -1, -1) - jnp.roll(field, 1, -1))


def neighbours(padded):
    middle = inner(padded)
    total = padded[..., 2:, 1:-1, :] + padded[..., :-2, 1:-1, :]
    total = total + padded[..., 1:-1, 2:, :] + padded[..., 1:-1, :-2, :]
    return total + jnp.roll(middle, 1, -1) + jnp.roll(middle, -1, -1)


def gradient_of(padded):
    middle = inner(padded)
    return jnp.stack([along_x(padded), along_y(middle), along_z(padded)])


def predict(flow_padded):
    velocity_padded = flow_padded[:3]
    pressure_padded = flow_padded[3]
    current = inner(velocity_padded)
    laplace = neighbours(velocity_padded) - 6.0 * current
    advect = current[0] * along_x(velocity_padded)
    return current + step_size * (viscosity * laplace - advect) - gradient_of(pressure_padded)


def kernel_box_cells(anchors, box_x, box_z, box_y):
    steps_x = jnp.arange(box_x, dtype=jnp.int32)
    steps_z = jnp.arange(box_z, dtype=jnp.int32)
    steps_y = jnp.arange(box_y, dtype=jnp.int32)
    cell_x = anchors[:, 0, None, None, None] + steps_x[None, :, None, None]
    cell_z = anchors[:, 1, None, None, None] + steps_z[None, None, :, None]
    cell_y = anchors[:, 2, None, None, None] + steps_y[None, None, None, :]
    return (cell_x, cell_z, cell_y)


def walls(padded, vertical_dim):
    tile_index = lax.axis_index("yz")
    tile_total = lax.axis_size("yz")
    extent = padded.shape[vertical_dim]
    position = lax.broadcasted_iota(jnp.int32, padded.shape, vertical_dim)
    bottom_rim = jnp.logical_and(position == 0, tile_index == 0)
    top_rim = jnp.logical_and(position == extent - 1, tile_index == tile_total - 1)
    return jnp.where(jnp.logical_or(bottom_rim, top_rim), jnp.zeros((), padded.dtype), padded)


def pressure_cycle(pressure):
    padded = extended(pressure, (("gx", 0), ("yz", 1)), 1)
    return walls(padded, 1)


def body(velocity, old_pressure, delta_weight, marker_target, pair_owner, pair_grain, box_anchor):
    flow_fields = jnp.concatenate([velocity, old_pressure[None]], 0)
    flow_padded = walls(extended(flow_fields, (("gx", 1), ("yz", 2)), 1), 2)
    predicted = predict(flow_padded)
    anchors = box_anchor[0]
    owners = pair_owner[0, :, 0]
    grains = pair_grain[0]
    delta_weights = delta_weight[0]
    grain_slots = marker_target.shape[1]
    pair_total = anchors.shape[0]
    cell_x, cell_z, cell_y = kernel_box_cells(anchors, BX, BZ, BY)
    kernel_box_values = (
        predicted[:, cell_x, cell_z, cell_y].astype(jnp.bfloat16).reshape(3, pair_total, -1)
    )
    partial_force_value = jnp.einsum(
        "eky,iey->eik", delta_weights, kernel_box_values, preferred_element_type=jnp.float32
    )
    row_width = partial_force_value.shape[1] * partial_force_value.shape[2]
    flat_partial = partial_force_value.reshape(pair_total, row_width)
    targets = marker_target[0].reshape(grain_slots, row_width)
    slot_numbers = jnp.arange(grain_slots, dtype=jnp.int32)
    all_partial, all_owner, all_grain = (
        lax.all_gather(flat_partial, "yz", axis=0, tiled=True),
        lax.all_gather(owners, "yz", axis=0, tiled=True),
        lax.all_gather(grains, "yz", axis=0, tiled=True),
    )
    own_tile = lax.axis_index("yz")
    grain_keys = jnp.where(all_owner == own_tile, all_grain, grain_slots)
    select = (grain_keys[None, :] == slot_numbers[:, None]).astype(jnp.float32)
    summed = jnp.dot(
        select, all_partial, precision=lax.Precision.HIGHEST, preferred_element_type=jnp.float32
    )
    grain_force = (targets - summed).astype(jnp.bfloat16)
    all_force = lax.all_gather(grain_force, "yz", axis=0, tiled=True)
    marker_pair_force = jnp.take(all_force, owners * grain_slots + grains, axis=0)
    spread_force = jnp.einsum(
        "zwx,znw->nzx",
        delta_weights,
        marker_pair_force.reshape(pair_total, 3, -1),
        preferred_element_type=jnp.float32,
    )
    spread_force = spread_force.reshape(3, pair_total, BX, BZ, BY)
    forced_velocity = predicted + jnp.zeros_like(predicted).at[:, cell_x, cell_z, cell_y].add(
        spread_force
    )
    forced_padded = walls(extended(forced_velocity, (("gx", 1), ("yz", 2)), 1), 2)
    divergence = along_x(forced_padded[0]) + along_y(forced_velocity[1]) + along_z(forced_padded[2])
    first_padded = pressure_cycle(old_pressure)
    pressure = (neighbours(first_padded) - divergence) / 6.0
    pressure = (neighbours(pressure_cycle(pressure)) - divergence) / 6.0
    new_velocity = forced_velocity - gradient_of(pressure_cycle(pressure))
    return (new_velocity, pressure)


def solution(mesh):
    placed = (
        P(None, "gx", "yz", None),
        P("gx", "yz", None),
        P("gx", "yz", None, None),
        P("gx", "yz", None, None),
        P("gx", "yz", None),
        P("gx", "yz"),
        P("gx", "yz", None),
    )
    return jax.shard_map(
        body,
        mesh=mesh,
        in_specs=placed,
        out_specs=(P(None, "gx", "yz", None), P("gx", "yz", None)),
        check_vma=False,
    )
```

profile of v0, /device:TPU:7, one launch (start us, length us, event | category | flops | bytes accessed | tf_op | source)
XLA Modules:
  0.0 358.6 jit_solution(16332044363483749540)
XLA Ops:
  7.2 0.9 pad_maximum_fusion.6
  8.2 2.5 collective-permute-start
  10.6 0.7 copy.560
  11.3 0.6 clamp_shift-left_fusion.1
  12.1 0.6 clamp_shift-left_fusion
  12.8 0.2 or_or_fusion
  13.0 0.2 reshape.255
  13.3 1.9 collective-permute-done.1
  15.5 6.4 %collective-permute-start.3 = (f32[4,34,1,128]{3,0,2,1:T(4,128)S(1)}, f32[4,34,1,128]{3,0,2,1:T(4,128)S(1)}, u32[]{:S(2)}, u32[]{:S(2)}) collective-permute-start(f32[4,34,1,128]{3,0,2,1:T(4,128)S(1)} %copy.535), channel_id=1, source_target_pairs={{1,0},{2,1},{3,2},{4,3},{5,4},{6,5},{7,6},{8,7},{9,8},{10,9},{11,1... | collective-permute-start | bytes 208904 | tf_op jit(solution)/shard_map/ppermute | solution.py:22
  21.9 2.5 collective-permute-done.2
  24.5 1.3 maximum_select_fusion
  25.9 0.9 fusion.52
  26.8 0.3 slice_reduce_fusion.3
  27.1 0.9 fusion.26
  28.0 1.2 fusion.43
  29.2 1.5 fusion.44
  30.6 0.7 fusion.27
  31.4 0.9 copy.491
  32.2 0.9 copy.493
  33.1 1.5 copy_bitcast_fusion.6
  34.6 1.3 copy_bitcast_fusion.5
  36.2 1.6 fusion.11
  37.9 17.1 %copy.528 = f32[3,32,16,128]{0,3,2,1:T(8,128)} copy(f32[3,32,16,128]{3,2,1,0:T(8,128)} %fusion.11) | data formatting | bytes 1572864
  54.9 43.8 %gather_fusion = bf16[4096,3]{1,0:T(8,128)(2,1)S(1)} fusion(f32[3,32,16,128]{0,3,2,1:T(8,128)} %copy.528, s32[4096]{0:T(1024)S(1)} %reshape.255), kind=kCustom, calls=%fused_computation | custom fusion | bytes 98304 | tf_op jit(solution)/shard_map/gather | solution.py:101
  98.8 0.7 fusion.2
  99.5 0.6 copy.559
  100.2 1.1 collective-permute-start.4
  101.4 0.6 dynamic-slice
  102.8 15.8 %all-reduce.2 = (s32[1024]{0:T(1024)S(1)}, s32[1024]{0:T(1024)S(1)}) all-reduce(s32[1024]{0:T(1024)S(1)} %bitcast_dynamic-update-slice_fusion.1, s32[1024]{0:T(1024)S(1)} %bitcast_dynamic-update-slice_fusion), channel_id=3, replica_groups=mesh['gx'=8,'yz'=32] {'yz'}, use_global_device_ids=true, to_apply=%add.1 | all-reduce | flops 2048 | bytes 16384 | tf_op jit(solution)/shard_map/all_gather | solution.py:113
  119.1 1.0 collective-permute-start.6
  120.1 3.9 %collective-permute-start.7 = (f32[34,1,128]{2,0,1:T(8,128)S(1)}, f32[34,1,128]{2,0,1:T(8,128)S(1)}, u32[]{:S(2)}, u32[]{:S(2)}) collective-permute-start(f32[34,1,128]{2,0,1:T(8,128)S(1)} %get-tuple-element.71), channel_id=1, source_target_pairs={{1,0},{2,1},{3,2},{4,3},{5,4},{6,5},{7,6},{8,7},{9,8},{10,9},{11,1... | collective-permute-start | bytes 52232 | tf_op jit(solution)/shard_map/ppermute | solution.py:22
  124.2 0.2 reshape.269
  124.5 0.7 collective-permute-done.6
  125.4 0.9 fusion.51
  126.3 45.6 %all-gather.4.cloned.1.call-done = f32[1024,384]{1,0:T(8,128)} async-done(((f32[32,384]{1,0:T(8,128)}), f32[1024,384]{1,0:T(8,128)}) %all-gather.4.cloned.1.call-update) | async-done | bytes 1572880 | tf_op jit(solution)/shard_map/all_gather | solution.py:111
  171.9 2.1 fusion
  174.0 36.3 %all_gather.15 = bf16[1024,384]{1,0:T(8,128)(2,1)S(1)} all-gather(bf16[32,384]{1,0:T(8,128)(2,1)S(1)} %fusion), channel_id=1, replica_groups=mesh['gx'=8,'yz'=32] {'yz'}, dimensions={0}, use_global_device_ids=true | all-gather | bytes 811008 | tf_op jit(solution)/shard_map/all_gather | solution.py:122
  210.3 0.6 gather_fusion.1
  210.9 0.4 convolution_bitcast_fusion
  211.3 2.0 copy.532
  213.3 42.0 %scatter_fusion = f32[3,65536]{0,1:T(8,128)} fusion(f32[3,65536]{0,1:T(8,128)} %bitcast.96, s32[4096]{0:T(1024)S(1)} %reshape.269, f32[4096,3]{1,0:T(8,128)} %bitcast.106), kind=kCustom, calls=%fused_computation.2 | custom fusion | flops 12288 | bytes 163840
  255.3 20.3 %slice_reduce_fusion = f32[65536]{0:T(1024)S(1)} fusion(f32[3,65536]{0,1:T(8,128)} %scatter_fusion), kind=kLoop, calls=%fused_computation.3 | loop fusion | bytes 524288 | tf_op jit(solution)/shard_map/slice | solution.py:135
  275.6 18.8 %copy.526 = f32[3,32,16,128]{3,2,1,0:T(8,128)S(1)} copy(f32[3,32,16,128]{0,3,2,1:T(8,128)} %bitcast.97) | data formatting | bytes 1572864 | tf_op jit(solution)/shard_map/scatter-add | solution.py:131
  294.4 17.8 %collective-permute-start.8 = (f32[3,1,16,128]{3,2,1,0:T(8,128)S(1)}, f32[3,1,16,128]{3,2,1,0:T(8,128)S(1)}, u32[]{:S(2)}, u32[]{:S(2)}) collective-permute-start(f32[3,1,16,128]{3,2,1,0:T(8,128)S(1)} %get-tuple-element.48), channel_id=1, source_target_pairs={{0,32},{32,64},{64,96},{96,128},{128,160},{160,192},{192,224},{224... | collective-permute-start | bytes 73736 | tf_op jit(solution)/shard_map/ppermute | solution.py:19
  312.4 0.8 collective-permute-done.8
  313.2 3.5 collective-permute-done.9
  316.9 4.8 %collective-permute-start.11 = (f32[3,34,1,128]{3,2,1,0:T(1,128)S(1)}, f32[3,34,1,128]{3,2,1,0:T(1,128)S(1)}, u32[]{:S(2)}, u32[]{:S(2)}) collective-permute-start(f32[3,34,1,128]{3,2,1,0:T(1,128)S(1)} %get-tuple-element.47), channel_id=1, source_target_pairs={{1,0},{2,1},{3,2},{4,3},{5,4},{6,5},{7,6},{8,7},{9,8},{10,9},{11,1... | collective-permute-start | bytes 156680 | tf_op jit(solution)/shard_map/ppermute | solution.py:22
  322.2 0.3 copy.514
  322.5 0.7 collective-permute-done.10
  323.5 0.7 copy-done.11
  324.3 0.5 fusion.24
  324.8 1.2 collective-permute-start.12
  325.9 0.8 collective-permute-done.12
  326.7 3.5 collective-permute-done.13
  330.3 5.1 %collective-permute-start.15 = (f32[34,1,128]{2,0,1:T(8,128)S(1)}, f32[34,1,128]{2,0,1:T(8,128)S(1)}, u32[]{:S(2)}, u32[]{:S(2)}) collective-permute-start(f32[34,1,128]{2,0,1:T(8,128)S(1)} %get-tuple-element.69), channel_id=1, source_target_pairs={{1,0},{2,1},{3,2},{4,3},{5,4},{6,5},{7,6},{8,7},{9,8},{10,9},{11,1... | collective-permute-start | bytes 52232 | tf_op jit(solution)/shard_map/ppermute | solution.py:22
  335.4 1.1 collective-permute-done.14
  336.9 0.2 fusion.17
  337.2 0.9 collective-permute-start.16
  338.1 0.8 collective-permute-done.16
  338.9 3.5 collective-permute-done.17
  342.5 5.2 %collective-permute-start.19 = (f32[34,1,128]{2,0,1:T(8,128)S(1)}, f32[34,1,128]{2,0,1:T(8,128)S(1)}, u32[]{:S(2)}, u32[]{:S(2)}) collective-permute-start(f32[34,1,128]{2,0,1:T(8,128)S(1)} %get-tuple-element.67), channel_id=1, source_target_pairs={{1,0},{2,1},{3,2},{4,3},{5,4},{6,5},{7,6},{8,7},{9,8},{10,9},{11,1... | collective-permute-start | bytes 52232 | tf_op jit(solution)/shard_map/ppermute | solution.py:22
  347.7 0.9 copy.527
  349.0 0.3 slice_reduce_fusion.1
  350.7 1.0 maximum_subtract_fusion
  (134 shorter events, 5.7 us)
Async XLA Ops:
  7.2 91.7 %copy-start = (bf16[1,32,128,128]{3,2,1,0:T(8,128)(2,1)S(1)}, bf16[1,32,128,128]{3,2,1,0:T(8,128)(2,1)}, u32[]{:S(2)}) copy-start(bf16[1,32,128,128]{3,2,1,0:T(8,128)(2,1)} %param.9) | copy-start | bytes 3145732
  7.2 8.0 %copy-start.3 = (f32[32,16,128]{2,1,0:T(8,128)S(1)}, f32[32,16,128]{2,1,0:T(8,128)}, u32[]{:S(2)}) copy-start(f32[32,16,128]{2,1,0:T(8,128)} %param.8) | copy-start | bytes 786436
  7.2 8.0 %copy-start.2 = (f32[3,32,16,128]{3,2,1,0:T(8,128)S(1)}, f32[3,32,16,128]{3,2,1,0:T(8,128)}, u32[]{:S(2)}) copy-start(f32[3,32,16,128]{3,2,1,0:T(8,128)} %param.7) | copy-start | bytes 2359300
  7.2 164.7 %all-gather.4.cloned.1.call-start = ((), (), s32[]{:S(2)}) async-start(), calls=%async_computation | async-start | bytes 1622016 | tf_op jit(solution)/shard_map/all_gather | solution.py:111
  8.2 5.1 %collective-permute-start = (f32[4,1,16,128]{3,2,1,0:T(8,128)S(1)}, f32[4,1,16,128]{3,2,1,0:T(8,128)S(1)}, u32[]{:S(2)}, u32[]{:S(2)}) collective-permute-start(f32[4,1,16,128]{3,2,1,0:T(8,128)S(1)} %get-tuple-element.44), channel_id=1, source_target_pairs={{0,32},{32,64},{64,96},{96,128},{128,160},{160,192},{192,224},{224... | collective-permute-start | bytes 98312 | tf_op jit(solution)/shard_map/ppermute | solution.py:19
  10.6 4.6 %collective-permute-start.1 = (f32[4,1,16,128]{3,2,1,0:T(8,128)S(1)}, f32[4,1,16,128]{3,2,1,0:T(8,128)S(1)}, u32[]{:S(2)}, u32[]{:S(2)}) collective-permute-start(f32[4,1,16,128]{3,2,1,0:T(8,128)S(1)} %get-tuple-element.45), channel_id=1, source_target_pairs={{32,0},{64,32},{96,64},{128,96},{160,128},{192,160},{224,192},{0,2... | collective-permute-start | bytes 98312 | tf_op jit(solution)/shard_map/ppermute | solution.py:22
  15.2 9.2 %copy-start.13 = (f32[4,1,16,128]{3,2,1,0:T(8,128)}, f32[4,1,16,128]{3,2,1,0:T(8,128)S(1)}, u32[]{:S(2)}) copy-start(f32[4,1,16,128]{3,2,1,0:T(8,128)S(1)} %collective-permute-done.1) | copy-start | bytes 98308
  15.3 9.0 %collective-permute-start.2 = (f32[4,34,1,128]{3,0,2,1:T(4,128)S(1)}, f32[4,34,1,128]{3,0,2,1:T(4,128)S(1)}, u32[]{:S(2)}, u32[]{:S(2)}) collective-permute-start(f32[4,34,1,128]{3,0,2,1:T(4,128)S(1)} %copy.534), channel_id=1, source_target_pairs={{0,1},{1,2},{2,3},{3,4},{4,5},{5,6},{6,7},{7,8},{8,9},{9,10},{10,1... | collective-permute-start | bytes 208904 | tf_op jit(solution)/shard_map/ppermute | solution.py:19
  15.5 9.0 %collective-permute-start.3 = (f32[4,34,1,128]{3,0,2,1:T(4,128)S(1)}, f32[4,34,1,128]{3,0,2,1:T(4,128)S(1)}, u32[]{:S(2)}, u32[]{:S(2)}) collective-permute-start(f32[4,34,1,128]{3,0,2,1:T(4,128)S(1)} %copy.535), channel_id=1, source_target_pairs={{1,0},{2,1},{3,2},{4,3},{5,4},{6,5},{7,6},{8,7},{9,8},{10,9},{11,1... | collective-permute-start | bytes 208904 | tf_op jit(solution)/shard_map/ppermute | solution.py:22
  21.9 4.0 %copy-start.16 = (pred[18]{0:T(512)(128)(4,1)}, pred[18]{0:T(512)(128)(4,1)S(1)}, u32[]{:S(2)}) copy-start(pred[18]{0:T(512)(128)(4,1)S(1)} %and_or_fusion) | copy-start | bytes 58
  33.1 2.9 copy-start.9
  33.1 2.9 copy-start.10
  33.1 3.1 copy-start.5
  33.1 3.1 copy-start.6
  33.1 3.1 copy-start.7
  33.1 3.1 copy-start.8
  98.7 1.5 copy-start.4
  98.7 2.6 copy-start.24
  98.7 3.9 %copy-start.23 = (s32[1,32,1]{1,2,0:T(1,128)S(1)}, s32[1,32,1]{1,2,0:T(1,128)}, u32[]{:S(2)}) copy-start(s32[1,32,1]{1,2,0:T(1,128)} %param.11) | copy-start | bytes 388
  98.8 4.0 %copy-start.22 = (s32[1,32]{1,0:T(1,128)S(1)}, s32[1,32]{1,0:T(1,128)}, u32[]{:S(2)}) copy-start(s32[1,32]{1,0:T(1,128)} %param.12) | copy-start | bytes 388
  98.8 19.9 %copy-start.19 = (s32[32,4]{0,1:T(4,128)S(1)}, s32[32,4]{0,1:T(4,128)}, u32[]{:S(2)}) copy-start(s32[32,4]{0,1:T(4,128)} %get-tuple-element.95) | copy-start | bytes 1540
  98.8 19.9 %copy-start.18 = (s32[32,4]{0,1:T(4,128)S(1)}, s32[32,4]{0,1:T(4,128)}, u32[]{:S(2)}) copy-start(s32[32,4]{0,1:T(4,128)} %get-tuple-element.88) | copy-start | bytes 1540
  98.8 19.9 %copy-start.15 = (s32[32,8]{0,1:T(8,128)S(1)}, s32[32,8]{0,1:T(8,128)}, u32[]{:S(2)}) copy-start(s32[32,8]{0,1:T(8,128)} %get-tuple-element.90) | copy-start | bytes 3076
  98.8 19.9 %copy-start.21 = (s32[3]{0:T(128)S(1)}, s32[3]{0:T(128)}, u32[]{:S(2)}) copy-start(s32[3]{0:T(128)} %constant.64) | copy-start | bytes 40
  98.8 20.0 %copy-start.20 = (s32[3]{0:T(128)S(1)}, s32[3]{0:T(128)}, u32[]{:S(2)}) copy-start(s32[3]{0:T(128)} %constant.67) | copy-start | bytes 40
  98.8 25.2 %copy-start.14 = (f32[1,32,3,128]{3,1,2,0:T(8,128)S(1)}, f32[1,32,3,128]{3,1,2,0:T(8,128)}, u32[]{:S(2)}) copy-start(f32[1,32,3,128]{3,1,2,0:T(8,128)} %param.10) | copy-start | bytes 147460
  99.5 25.7 %copy-start.17 = (pred[18]{0:T(512)(128)(4,1)S(1)}, pred[18]{0:T(512)(128)(4,1)}, u32[]{:S(2)}) copy-start(pred[18]{0:T(512)(128)(4,1)} %copy-done.16) | copy-start | bytes 58
  100.2 18.9 %collective-permute-start.4 = (f32[1,16,128]{2,0,1:T(1,128)S(1)}, f32[1,16,128]{2,0,1:T(1,128)S(1)}, u32[]{:S(2)}, u32[]{:S(2)}) collective-permute-start(f32[1,16,128]{2,0,1:T(1,128)S(1)} %bitcast.120), channel_id=1, source_target_pairs={{0,32},{32,64},{64,96},{96,128},{128,160},{160,192},{192,224},{224... | collective-permute-start | bytes 24584 | tf_op jit(solution)/shard_map/ppermute | solution.py:19
  101.4 17.7 %collective-permute-start.5 = (f32[1,16,128]{2,0,1:T(1,128)S(1)}, f32[1,16,128]{2,0,1:T(1,128)S(1)}, u32[]{:S(2)}, u32[]{:S(2)}) collective-permute-start(f32[1,16,128]{2,0,1:T(1,128)S(1)} %bitcast.119), channel_id=1, source_target_pairs={{32,0},{64,32},{96,64},{128,96},{160,128},{192,160},{224,192},{0,2... | collective-permute-start | bytes 24584 | tf_op jit(solution)/shard_map/ppermute | solution.py:22
  119.1 6.1 %collective-permute-start.6 = (f32[34,1,128]{2,0,1:T(8,128)S(1)}, f32[34,1,128]{2,0,1:T(8,128)S(1)}, u32[]{:S(2)}, u32[]{:S(2)}) collective-permute-start(f32[34,1,128]{2,0,1:T(8,128)S(1)} %get-tuple-element.70), channel_id=1, source_target_pairs={{0,1},{1,2},{2,3},{3,4},{4,5},{5,6},{6,7},{7,8},{8,9},{9,10},{10,1... | collective-permute-start | bytes 52232 | tf_op jit(solution)/shard_map/ppermute | solution.py:19
  120.1 5.1 %collective-permute-start.7 = (f32[34,1,128]{2,0,1:T(8,128)S(1)}, f32[34,1,128]{2,0,1:T(8,128)S(1)}, u32[]{:S(2)}, u32[]{:S(2)}) collective-permute-start(f32[34,1,128]{2,0,1:T(8,128)S(1)} %get-tuple-element.71), channel_id=1, source_target_pairs={{1,0},{2,1},{3,2},{4,3},{5,4},{6,5},{7,6},{8,7},{9,8},{10,9},{11,1... | collective-permute-start | bytes 52232 | tf_op jit(solution)/shard_map/ppermute | solution.py:22
  294.4 18.8 %collective-permute-start.8 = (f32[3,1,16,128]{3,2,1,0:T(8,128)S(1)}, f32[3,1,16,128]{3,2,1,0:T(8,128)S(1)}, u32[]{:S(2)}, u32[]{:S(2)}) collective-permute-start(f32[3,1,16,128]{3,2,1,0:T(8,128)S(1)} %get-tuple-element.48), channel_id=1, source_target_pairs={{0,32},{32,64},{64,96},{96,128},{128,160},{160,192},{192,224},{224... | collective-permute-start | bytes 73736 | tf_op jit(solution)/shard_map/ppermute | solution.py:19
  312.2 4.5 %collective-permute-start.9 = (f32[3,1,16,128]{3,2,1,0:T(8,128)S(1)}, f32[3,1,16,128]{3,2,1,0:T(8,128)S(1)}, u32[]{:S(2)}, u32[]{:S(2)}) collective-permute-start(f32[3,1,16,128]{3,2,1,0:T(8,128)S(1)} %get-tuple-element.49), channel_id=1, source_target_pairs={{32,0},{64,32},{96,64},{128,96},{160,128},{192,160},{224,192},{0,2... | collective-permute-start | bytes 73736 | tf_op jit(solution)/shard_map/ppermute | solution.py:22
  316.8 6.4 %collective-permute-start.10 = (f32[3,34,1,128]{3,2,1,0:T(1,128)S(1)}, f32[3,34,1,128]{3,2,1,0:T(1,128)S(1)}, u32[]{:S(2)}, u32[]{:S(2)}) collective-permute-start(f32[3,34,1,128]{3,2,1,0:T(1,128)S(1)} %get-tuple-element.46), channel_id=1, source_target_pairs={{0,1},{1,2},{2,3},{3,4},{4,5},{5,6},{6,7},{7,8},{8,9},{9,10},{10,1... | collective-permute-start | bytes 156680 | tf_op jit(solution)/shard_map/ppermute | solution.py:19
  316.9 6.3 %collective-permute-start.11 = (f32[3,34,1,128]{3,2,1,0:T(1,128)S(1)}, f32[3,34,1,128]{3,2,1,0:T(1,128)S(1)}, u32[]{:S(2)}, u32[]{:S(2)}) collective-permute-start(f32[3,34,1,128]{3,2,1,0:T(1,128)S(1)} %get-tuple-element.47), channel_id=1, source_target_pairs={{1,0},{2,1},{3,2},{4,3},{5,4},{6,5},{7,6},{8,7},{9,8},{10,9},{11,1... | collective-permute-start | bytes 156680 | tf_op jit(solution)/shard_map/ppermute | solution.py:22
  323.2 1.0 copy-start.11
  323.3 1.0 copy-start.12
  324.8 2.0 collective-permute-start.12
  325.9 4.3 %collective-permute-start.13 = (f32[1,16,128]{2,0,1:T(1,128)S(1)}, f32[1,16,128]{2,0,1:T(1,128)S(1)}, u32[]{:S(2)}, u32[]{:S(2)}) collective-permute-start(f32[1,16,128]{2,0,1:T(1,128)S(1)} %get-tuple-element.75), channel_id=1, source_target_pairs={{32,0},{64,32},{96,64},{128,96},{160,128},{192,160},{224,192},{0,2... | collective-permute-start | bytes 24584 | tf_op jit(solution)/shard_map/ppermute | solution.py:22
  330.2 6.3 %collective-permute-start.14 = (f32[34,1,128]{2,0,1:T(8,128)S(1)}, f32[34,1,128]{2,0,1:T(8,128)S(1)}, u32[]{:S(2)}, u32[]{:S(2)}) collective-permute-start(f32[34,1,128]{2,0,1:T(8,128)S(1)} %get-tuple-element.68), channel_id=1, source_target_pairs={{0,1},{1,2},{2,3},{3,4},{4,5},{5,6},{6,7},{7,8},{8,9},{9,10},{10,1... | collective-permute-start | bytes 52232 | tf_op jit(solution)/shard_map/ppermute | solution.py:19
  330.3 6.2 %collective-permute-start.15 = (f32[34,1,128]{2,0,1:T(8,128)S(1)}, f32[34,1,128]{2,0,1:T(8,128)S(1)}, u32[]{:S(2)}, u32[]{:S(2)}) collective-permute-start(f32[34,1,128]{2,0,1:T(8,128)S(1)} %get-tuple-element.69), channel_id=1, source_target_pairs={{1,0},{2,1},{3,2},{4,3},{5,4},{6,5},{7,6},{8,7},{9,8},{10,9},{11,1... | collective-permute-start | bytes 52232 | tf_op jit(solution)/shard_map/ppermute | solution.py:22
  337.2 1.7 collective-permute-start.16
  338.1 4.3 %collective-permute-start.17 = (f32[1,16,128]{2,0,1:T(1,128)S(1)}, f32[1,16,128]{2,0,1:T(1,128)S(1)}, u32[]{:S(2)}, u32[]{:S(2)}) collective-permute-start(f32[1,16,128]{2,0,1:T(1,128)S(1)} %get-tuple-element.73), channel_id=1, source_target_pairs={{32,0},{64,32},{96,64},{128,96},{160,128},{192,160},{224,192},{0,2... | collective-permute-start | bytes 24584 | tf_op jit(solution)/shard_map/ppermute | solution.py:22
  342.4 6.4 %collective-permute-start.18 = (f32[34,1,128]{2,0,1:T(8,128)S(1)}, f32[34,1,128]{2,0,1:T(8,128)S(1)}, u32[]{:S(2)}, u32[]{:S(2)}) collective-permute-start(f32[34,1,128]{2,0,1:T(8,128)S(1)} %get-tuple-element.66), channel_id=1, source_target_pairs={{0,1},{1,2},{2,3},{3,4},{4,5},{5,6},{6,7},{7,8},{8,9},{9,10},{10,1... | collective-permute-start | bytes 52232 | tf_op jit(solution)/shard_map/ppermute | solution.py:19
  342.5 6.3 %collective-permute-start.19 = (f32[34,1,128]{2,0,1:T(8,128)S(1)}, f32[34,1,128]{2,0,1:T(8,128)S(1)}, u32[]{:S(2)}, u32[]{:S(2)}) collective-permute-start(f32[34,1,128]{2,0,1:T(8,128)S(1)} %get-tuple-element.67), channel_id=1, source_target_pairs={{1,0},{2,1},{3,2},{4,3},{5,4},{6,5},{7,6},{8,7},{9,8},{10,9},{11,1... | collective-permute-start | bytes 52232 | tf_op jit(solution)/shard_map/ppermute | solution.py:22
  350.5 1.2 copy-start.1
Sparse Core Ops, SparseCore 0:
  100.3 71.5 all-gather.3
where the time goes:
time: 360 us; the launch traced here: 359 us
  local copies, waits for them, and re-layouts  120 us (33%)
  waiting for transfers between devices  65.7 us (18%)
  blocking collectives  52.1 us (14%)
  other arithmetic  51.9 us (14%)
  starting transfers between devices  50.3 us (14%)
  between operations  15.5 us (4%)
    all_gather x1, waiting for transfers between devices, body(): lax.all_gather(flat_partial, 'yz', axis=0, tiled=True)  45.6 us
    gather x1, local copies, waits for them, and re-layouts, body(): predicted[:, cell_x, cell_z, cell_y].astype(jnp.bfloat16)  43.8 us
    unnamed x4, other arithmetic  42.2 us
    all_gather x1, blocking collectives, body(): all_force = lax.all_gather(grain_force, 'yz', axis=0, tiled=True)  36.3 us
    ppermute x10, starting transfers between devices, extended(): lax.ppermute(lax.slice_in_dim(block, 0, width, axis=dim), axis, backward)  25.4 us
    ppermute x10, starting transfers between devices, extended(): lax.ppermute(lax.slice_in_dim(block, block.shape[dim] - width, None, axis...  24.9 us
    unnamed x69, local copies, waits for them, and re-layouts  22 us
    slice x1, local copies, waits for them, and re-layouts, body(): forced_velocity[1]  20.3 us
  transfers between devices with their start and end apart: 21, of which 13 were waited for; matrix products, arithmetic and copies ran while one was open for 2% of the time, Pallas kernels for 0%

commit v1 on v0

--- a/solution.py
+++ b/solution.py
@@ -108,7 +108,9 @@
     targets = marker_target[0].reshape(grain_slots, row_width)
     slot_numbers = jnp.arange(grain_slots, dtype=jnp.int32)
     all_partial, all_owner, all_grain = (
-        lax.all_gather(flat_partial, "yz", axis=0, tiled=True),
+        jnp.concatenate(
+            lax.all_to_all(jnp.stack([flat_partial] * lax.axis_size("yz")), "yz", 0, 0), axis=0
+        ),
         lax.all_gather(owners, "yz", axis=0, tiled=True),
         lax.all_gather(grains, "yz", axis=0, tiled=True),
     )

time: 360 us -> 331 us (0.919)
  waiting for transfers between devices: 65.7 us -> 19.3 us
  blocking collectives: 52.1 us -> 75.9 us
  between operations: 15.5 us -> 2.03 us
  starting transfers between devices: 50.3 us -> 56.8 us
    all_gather x1 -> x0, waiting for transfers between devices: 45.6 us -> none  [body(): lax.all_gather(flat_partial, 'yz', axis=0, tiled=True)]
    all_gather x1, blocking collectives: 15.8 us -> 38.2 us  [body(): lax.all_gather(grains, 'yz', axis=0, tiled=True)]
    all_to_all x0 -> x1, starting transfers between devices: none -> 7.62 us  [body(): lax.all_to_all(jnp.stack([flat_partial] * lax.axis_size('yz')), 'yz', 0, 0)]
  transfers between devices with their start and end apart: 21 -> 21, of which waited for: 13 -> 12; matrix products, arithmetic and copies ran while one was open for 2% -> 2% of each run, Pallas kernels for 0% -> 0%
where the time goes in v1:
time: 331 us; the launch traced here: 330 us
  local copies, waits for them, and re-layouts  122 us (37%)
  blocking collectives  75.9 us (23%)
  starting transfers between devices  56.8 us (17%)
  other arithmetic  51.9 us (16%)
  waiting for transfers between devices  19.3 us (6%)
    gather x1, local copies, waits for them, and re-layouts, body(): predicted[:, cell_x, cell_z, cell_y].astype(jnp.bfloat16)  43.8 us
    unnamed x4, other arithmetic  42.2 us
    all_gather x1, blocking collectives, body(): lax.all_gather(grains, 'yz', axis=0, tiled=True)  38.2 us
    all_gather x1, blocking collectives, body(): all_force = lax.all_gather(grain_force, 'yz', axis=0, tiled=True)  37.7 us
    ppermute x10, starting transfers between devices, extended(): lax.ppermute(lax.slice_in_dim(block, 0, width, axis=dim), axis, backward)  25.4 us
    ppermute x10, starting transfers between devices, extended(): lax.ppermute(lax.slice_in_dim(block, block.shape[dim] - width, None, axis...  23.8 us
    unnamed x69, local copies, waits for them, and re-layouts  22 us
    slice x1, local copies, waits for them, and re-layouts, body(): forced_velocity[1]  20.3 us
  transfers between devices with their start and end apart: 21, of which 12 were waited for; matrix products, arithmetic and copies ran while one was open for 2% of the time, Pallas kernels for 0%

profile of v1, /device:TPU:7, one launch (start us, length us, event | category | flops | bytes accessed | tf_op | source)
XLA Modules:
  0.0 330.0 jit_solution(365592588748647591)
XLA Ops:
  0.7 0.9 pad_maximum_fusion.6
  1.6 2.5 collective-permute-start
  4.1 0.7 copy.560
  4.8 0.6 clamp_shift-left_fusion.1
  5.5 0.6 clamp_shift-left_fusion
  6.4 0.2 reshape.257
  6.7 1.9 collective-permute-done.1
  8.9 6.4 %collective-permute-start.3 = (f32[4,34,1,128]{3,0,2,1:T(4,128)S(1)}, f32[4,34,1,128]{3,0,2,1:T(4,128)S(1)}, u32[]{:S(2)}, u32[]{:S(2)}) collective-permute-start(f32[4,34,1,128]{3,0,2,1:T(4,128)S(1)} %copy.535), channel_id=1, source_target_pairs={{1,0},{2,1},{3,2},{4,3},{5,4},{6,5},{7,6},{8,7},{9,8},{10,9},{11,1... | collective-permute-start | bytes 208904 | tf_op jit(solution)/shard_map/ppermute | solution.py:22
  15.3 2.5 collective-permute-done.2
  18.0 1.3 maximum_select_fusion
  19.4 0.9 fusion.52
  20.3 0.3 slice_reduce_fusion.3
  20.6 0.9 fusion.26
  21.4 1.2 fusion.43
  22.6 1.5 fusion.44
  24.1 0.7 fusion.27
  24.8 0.9 copy.491
  25.7 0.9 copy.493
  26.6 1.5 copy_bitcast_fusion.6
  28.1 1.3 copy_bitcast_fusion.5
  29.7 1.6 fusion.11
  31.3 17.1 %copy.528 = f32[3,32,16,128]{0,3,2,1:T(8,128)} copy(f32[3,32,16,128]{3,2,1,0:T(8,128)} %fusion.11) | data formatting | bytes 1572864
  48.5 43.8 %gather_fusion = bf16[4096,3]{1,0:T(8,128)(2,1)S(1)} fusion(f32[3,32,16,128]{0,3,2,1:T(8,128)} %copy.528, s32[4096]{0:T(1024)S(1)} %reshape.257), kind=kCustom, calls=%fused_computation | custom fusion | bytes 98304 | tf_op jit(solution)/shard_map/gather | solution.py:101
  92.3 0.7 fusion.2
  93.0 1.4 stack.26
  94.4 7.6 %all-to-all-start = ((f32[32,32,384]{2,1,0:T(8,128)}), f32[32,32,384]{2,1,0:T(8,128)S(1)}, u32[]{:S(2)}, u32[]{:S(2)}) async-start(f32[32,32,384]{2,1,0:T(8,128)} %stack.26), calls=%async_computation | async-start | bytes 3145728 | tf_op jit(solution)/shard_map/all_to_all | solution.py:112
  102.1 2.2 collective-permute-start.4
  104.3 0.6 dynamic-slice
  105.7 38.2 %all-reduce.2 = (s32[1024]{0:T(1024)S(1)}, s32[1024]{0:T(1024)S(1)}) all-reduce(s32[1024]{0:T(1024)S(1)} %bitcast_dynamic-update-slice_fusion.1, s32[1024]{0:T(1024)S(1)} %bitcast_dynamic-update-slice_fusion), channel_id=3, replica_groups=mesh['gx'=8,'yz'=32] {'yz'}, use_global_device_ids=true, to_apply=%add.1 | all-reduce | flops 2048 | bytes 16384 | tf_op jit(solution)/shard_map/all_gather | solution.py:115
  144.4 1.2 collective-permute-start.6
  145.6 3.6 %collective-permute-start.7 = (f32[34,1,128]{2,0,1:T(8,128)S(1)}, f32[34,1,128]{2,0,1:T(8,128)S(1)}, u32[]{:S(2)}, u32[]{:S(2)}) collective-permute-start(f32[34,1,128]{2,0,1:T(8,128)S(1)} %get-tuple-element.71), channel_id=1, source_target_pairs={{1,0},{2,1},{3,2},{4,3},{5,4},{6,5},{7,6},{8,7},{9,8},{10,9},{11,1... | collective-permute-start | bytes 52232 | tf_op jit(solution)/shard_map/ppermute | solution.py:22
  149.3 0.7 copy.496
  150.7 0.9 fusion.51
  151.5 1.5 fusion
  153.1 37.7 %all_gather.11 = bf16[1024,384]{1,0:T(8,128)(2,1)S(1)} all-gather(bf16[32,384]{1,0:T(8,128)(2,1)S(1)} %fusion), channel_id=1, replica_groups=mesh['gx'=8,'yz'=32] {'yz'}, dimensions={0}, use_global_device_ids=true | all-gather | bytes 811008 | tf_op jit(solution)/shard_map/all_gather | solution.py:124
  190.8 0.6 gather_fusion.1
  191.4 0.4 convolution_bitcast_fusion
  191.8 2.0 copy.532
  193.8 42.0 %scatter_fusion = f32[3,65536]{0,1:T(8,128)} fusion(f32[3,65536]{0,1:T(8,128)} %bitcast.97, s32[4096]{0:T(1024)S(1)} %reshape.271, f32[4096,3]{1,0:T(8,128)} %bitcast.108), kind=kCustom, calls=%fused_computation.2 | custom fusion | flops 12288 | bytes 163840
  235.8 20.3 %slice_reduce_fusion = f32[65536]{0:T(1024)S(1)} fusion(f32[3,65536]{0,1:T(8,128)} %scatter_fusion), kind=kLoop, calls=%fused_computation.3 | loop fusion | bytes 524288 | tf_op jit(solution)/shard_map/slice | solution.py:137
  256.1 18.8 %copy.526 = f32[3,32,16,128]{3,2,1,0:T(8,128)S(1)} copy(f32[3,32,16,128]{0,3,2,1:T(8,128)} %bitcast.98) | data formatting | bytes 1572864 | tf_op jit(solution)/shard_map/scatter-add | solution.py:133
  274.9 14.9 %collective-permute-start.8 = (f32[3,1,16,128]{3,2,1,0:T(8,128)S(1)}, f32[3,1,16,128]{3,2,1,0:T(8,128)S(1)}, u32[]{:S(2)}, u32[]{:S(2)}) collective-permute-start(f32[3,1,16,128]{3,2,1,0:T(8,128)S(1)} %get-tuple-element.48), channel_id=1, source_target_pairs={{0,32},{32,64},{64,96},{96,128},{128,160},{160,192},{192,224},{224... | collective-permute-start | bytes 73736 | tf_op jit(solution)/shard_map/ppermute | solution.py:19
  289.8 0.8 collective-permute-start.9
  290.7 0.5 collective-permute-done.8
  291.3 3.0 collective-permute-done.9
  294.4 1.2 collective-permute-start.10
  295.6 3.7 %collective-permute-start.11 = (f32[3,34,1,128]{3,2,1,0:T(1,128)S(1)}, f32[3,34,1,128]{3,2,1,0:T(1,128)S(1)}, u32[]{:S(2)}, u32[]{:S(2)}) collective-permute-start(f32[3,34,1,128]{3,2,1,0:T(1,128)S(1)} %get-tuple-element.47), channel_id=1, source_target_pairs={{1,0},{2,1},{3,2},{4,3},{5,4},{6,5},{7,6},{8,7},{9,8},{10,9},{11,1... | collective-permute-start | bytes 156680 | tf_op jit(solution)/shard_map/ppermute | solution.py:22
  299.8 0.3 copy.514
  300.1 1.5 collective-permute-done.10
  301.9 0.7 copy-done.11
  302.7 0.5 fusion.24
  303.2 0.7 collective-permute-start.12
  303.9 0.8 collective-permute-done.12
  304.7 3.5 %collective-permute-done.13 = f32[1,16,128]{2,0,1:T(1,128)S(1)} collective-permute-done((f32[1,16,128]{2,0,1:T(1,128)S(1)}, f32[1,16,128]{2,0,1:T(1,128)S(1)}, u32[]{:S(2)}, u32[]{:S(2)}) %collective-permute-start.13) | collective-permute-done | bytes 8224 | tf_op jit(solution)/shard_map/ppermute | solution.py:22
  308.3 5.4 %collective-permute-start.15 = (f32[34,1,128]{2,0,1:T(8,128)S(1)}, f32[34,1,128]{2,0,1:T(8,128)S(1)}, u32[]{:S(2)}, u32[]{:S(2)}) collective-permute-start(f32[34,1,128]{2,0,1:T(8,128)S(1)} %get-tuple-element.69), channel_id=1, source_target_pairs={{1,0},{2,1},{3,2},{4,3},{5,4},{6,5},{7,6},{8,7},{9,8},{10,9},{11,1... | collective-permute-start | bytes 52232 | tf_op jit(solution)/shard_map/ppermute | solution.py:22
  313.7 0.9 collective-permute-done.14
  315.0 0.2 fusion.17
  315.3 0.9 collective-permute-start.16
  316.2 0.8 collective-permute-done.16
  317.0 3.5 %collective-permute-done.17 = f32[1,16,128]{2,0,1:T(1,128)S(1)} collective-permute-done((f32[1,16,128]{2,0,1:T(1,128)S(1)}, f32[1,16,128]{2,0,1:T(1,128)S(1)}, u32[]{:S(2)}, u32[]{:S(2)}) %collective-permute-start.17) | collective-permute-done | bytes 8224 | tf_op jit(solution)/shard_map/ppermute | solution.py:22
  320.6 5.4 %collective-permute-start.19 = (f32[34,1,128]{2,0,1:T(8,128)S(1)}, f32[34,1,128]{2,0,1:T(8,128)S(1)}, u32[]{:S(2)}, u32[]{:S(2)}) collective-permute-start(f32[34,1,128]{2,0,1:T(8,128)S(1)} %get-tuple-element.67), channel_id=1, source_target_pairs={{1,0},{2,1},{3,2},{4,3},{5,4},{6,5},{7,6},{8,7},{9,8},{10,9},{11,1... | collective-permute-start | bytes 52232 | tf_op jit(solution)/shard_map/ppermute | solution.py:22
  326.0 0.9 copy.527
  327.3 0.3 slice_reduce_fusion.1
  329.0 1.0 maximum_subtract_fusion
  (134 shorter events, 6.1 us)
Async XLA Ops:
  0.6 91.7 %copy-start = (bf16[1,32,128,128]{3,2,1,0:T(8,128)(2,1)S(1)}, bf16[1,32,128,128]{3,2,1,0:T(8,128)(2,1)}, u32[]{:S(2)}) copy-start(bf16[1,32,128,128]{3,2,1,0:T(8,128)(2,1)} %param.9) | copy-start | bytes 3145732
  0.6 8.0 %copy-start.3 = (f32[32,16,128]{2,1,0:T(8,128)S(1)}, f32[32,16,128]{2,1,0:T(8,128)}, u32[]{:S(2)}) copy-start(f32[32,16,128]{2,1,0:T(8,128)} %param.8) | copy-start | bytes 786436
  0.7 8.0 %copy-start.2 = (f32[3,32,16,128]{3,2,1,0:T(8,128)S(1)}, f32[3,32,16,128]{3,2,1,0:T(8,128)}, u32[]{:S(2)}) copy-start(f32[3,32,16,128]{3,2,1,0:T(8,128)} %param.7) | copy-start | bytes 2359300
  1.6 5.1 %collective-permute-start = (f32[4,1,16,128]{3,2,1,0:T(8,128)S(1)}, f32[4,1,16,128]{3,2,1,0:T(8,128)S(1)}, u32[]{:S(2)}, u32[]{:S(2)}) collective-permute-start(f32[4,1,16,128]{3,2,1,0:T(8,128)S(1)} %get-tuple-element.44), channel_id=1, source_target_pairs={{0,32},{32,64},{64,96},{96,128},{128,160},{160,192},{192,224},{224... | collective-permute-start | bytes 98312 | tf_op jit(solution)/shard_map/ppermute | solution.py:19
  4.1 4.6 %collective-permute-start.1 = (f32[4,1,16,128]{3,2,1,0:T(8,128)S(1)}, f32[4,1,16,128]{3,2,1,0:T(8,128)S(1)}, u32[]{:S(2)}, u32[]{:S(2)}) collective-permute-start(f32[4,1,16,128]{3,2,1,0:T(8,128)S(1)} %get-tuple-element.45), channel_id=1, source_target_pairs={{32,0},{64,32},{96,64},{128,96},{160,128},{192,160},{224,192},{0,2... | collective-permute-start | bytes 98312 | tf_op jit(solution)/shard_map/ppermute | solution.py:22
  8.6 9.2 %copy-start.13 = (f32[4,1,16,128]{3,2,1,0:T(8,128)}, f32[4,1,16,128]{3,2,1,0:T(8,128)S(1)}, u32[]{:S(2)}) copy-start(f32[4,1,16,128]{3,2,1,0:T(8,128)S(1)} %collective-permute-done.1) | copy-start | bytes 98308
  8.8 9.0 %collective-permute-start.2 = (f32[4,34,1,128]{3,0,2,1:T(4,128)S(1)}, f32[4,34,1,128]{3,0,2,1:T(4,128)S(1)}, u32[]{:S(2)}, u32[]{:S(2)}) collective-permute-start(f32[4,34,1,128]{3,0,2,1:T(4,128)S(1)} %copy.534), channel_id=1, source_target_pairs={{0,1},{1,2},{2,3},{3,4},{4,5},{5,6},{6,7},{7,8},{8,9},{9,10},{10,1... | collective-permute-start | bytes 208904 | tf_op jit(solution)/shard_map/ppermute | solution.py:19
  8.9 9.0 %collective-permute-start.3 = (f32[4,34,1,128]{3,0,2,1:T(4,128)S(1)}, f32[4,34,1,128]{3,0,2,1:T(4,128)S(1)}, u32[]{:S(2)}, u32[]{:S(2)}) collective-permute-start(f32[4,34,1,128]{3,0,2,1:T(4,128)S(1)} %copy.535), channel_id=1, source_target_pairs={{1,0},{2,1},{3,2},{4,3},{5,4},{6,5},{7,6},{8,7},{9,8},{10,9},{11,1... | collective-permute-start | bytes 208904 | tf_op jit(solution)/shard_map/ppermute | solution.py:22
  15.3 4.0 %copy-start.16 = (pred[18]{0:T(512)(128)(4,1)}, pred[18]{0:T(512)(128)(4,1)S(1)}, u32[]{:S(2)}) copy-start(pred[18]{0:T(512)(128)(4,1)S(1)} %and_or_fusion) | copy-start | bytes 58
  26.6 2.9 copy-start.9
  26.6 2.9 copy-start.10
  26.6 3.1 copy-start.5
  26.6 3.1 copy-start.6
  26.6 3.1 copy-start.7
  26.6 3.1 copy-start.8
  94.4 7.7 %copy-start.4 = (f32[32,16,128]{2,1,0:T(8,128)S(1)}, f32[32,16,128]{2,1,0:T(8,128)}, u32[]{:S(2)}) copy-start(f32[32,16,128]{2,1,0:T(8,128)} %param.8) | copy-start | bytes 786436
  94.4 9.9 %copy-start.24 = (u32[256]{0:T(256)S(1)}, u32[256]{0:T(256)}, u32[]{:S(2)}) copy-start(u32[256]{0:T(256)} %constant.93) | copy-start | bytes 3076
  94.4 11.1 %copy-start.23 = (s32[1,32,1]{1,2,0:T(1,128)S(1)}, s32[1,32,1]{1,2,0:T(1,128)}, u32[]{:S(2)}) copy-start(s32[1,32,1]{1,2,0:T(1,128)} %param.11) | copy-start | bytes 388
  94.4 11.3 %copy-start.22 = (s32[1,32]{1,0:T(1,128)S(1)}, s32[1,32]{1,0:T(1,128)}, u32[]{:S(2)}) copy-start(s32[1,32]{1,0:T(1,128)} %param.12) | copy-start | bytes 388
  94.4 49.5 %copy-start.19 = (s32[32,4]{0,1:T(4,128)S(1)}, s32[32,4]{0,1:T(4,128)}, u32[]{:S(2)}) copy-start(s32[32,4]{0,1:T(4,128)} %get-tuple-element.95) | copy-start | bytes 1540
  94.4 49.5 %copy-start.18 = (s32[32,4]{0,1:T(4,128)S(1)}, s32[32,4]{0,1:T(4,128)}, u32[]{:S(2)}) copy-start(s32[32,4]{0,1:T(4,128)} %get-tuple-element.88) | copy-start | bytes 1540
  94.4 49.5 %copy-start.15 = (s32[32,8]{0,1:T(8,128)S(1)}, s32[32,8]{0,1:T(8,128)}, u32[]{:S(2)}) copy-start(s32[32,8]{0,1:T(8,128)} %get-tuple-element.90) | copy-start | bytes 3076
  94.4 49.6 %copy-start.21 = (s32[3]{0:T(128)S(1)}, s32[3]{0:T(128)}, u32[]{:S(2)}) copy-start(s32[3]{0:T(128)} %constant.64) | copy-start | bytes 40
  94.4 49.7 %copy-start.20 = (s32[3]{0:T(128)S(1)}, s32[3]{0:T(128)}, u32[]{:S(2)}) copy-start(s32[3]{0:T(128)} %constant.67) | copy-start | bytes 40
  94.4 57.1 %all-to-all-start = ((f32[32,32,384]{2,1,0:T(8,128)}), f32[32,32,384]{2,1,0:T(8,128)S(1)}, u32[]{:S(2)}, u32[]{:S(2)}) async-start(f32[32,32,384]{2,1,0:T(8,128)} %stack.26), calls=%async_computation | async-start | bytes 3145728 | tf_op jit(solution)/shard_map/all_to_all | solution.py:112
  102.1 47.2 %copy-start.14 = (f32[1,32,3,128]{3,1,2,0:T(8,128)S(1)}, f32[1,32,3,128]{3,1,2,0:T(8,128)}, u32[]{:S(2)}) copy-start(f32[1,32,3,128]{3,1,2,0:T(8,128)} %param.10) | copy-start | bytes 147460
  102.1 48.3 %copy-start.17 = (pred[18]{0:T(512)(128)(4,1)S(1)}, pred[18]{0:T(512)(128)(4,1)}, u32[]{:S(2)}) copy-start(pred[18]{0:T(512)(128)(4,1)} %copy-done.16) | copy-start | bytes 58
  102.1 42.3 %collective-permute-start.4 = (f32[1,16,128]{2,0,1:T(1,128)S(1)}, f32[1,16,128]{2,0,1:T(1,128)S(1)}, u32[]{:S(2)}, u32[]{:S(2)}) collective-permute-start(f32[1,16,128]{2,0,1:T(1,128)S(1)} %bitcast.122), channel_id=1, source_target_pairs={{0,32},{32,64},{64,96},{96,128},{128,160},{160,192},{192,224},{224... | collective-permute-start | bytes 24584 | tf_op jit(solution)/shard_map/ppermute | solution.py:19
  104.2 40.1 %collective-permute-start.5 = (f32[1,16,128]{2,0,1:T(1,128)S(1)}, f32[1,16,128]{2,0,1:T(1,128)S(1)}, u32[]{:S(2)}, u32[]{:S(2)}) collective-permute-start(f32[1,16,128]{2,0,1:T(1,128)S(1)} %bitcast.121), channel_id=1, source_target_pairs={{32,0},{64,32},{96,64},{128,96},{160,128},{192,160},{224,192},{0,2... | collective-permute-start | bytes 24584 | tf_op jit(solution)/shard_map/ppermute | solution.py:22
  144.4 6.0 %collective-permute-start.6 = (f32[34,1,128]{2,0,1:T(8,128)S(1)}, f32[34,1,128]{2,0,1:T(8,128)S(1)}, u32[]{:S(2)}, u32[]{:S(2)}) collective-permute-start(f32[34,1,128]{2,0,1:T(8,128)S(1)} %get-tuple-element.70), channel_id=1, source_target_pairs={{0,1},{1,2},{2,3},{3,4},{4,5},{5,6},{6,7},{7,8},{8,9},{9,10},{10,1... | collective-permute-start | bytes 52232 | tf_op jit(solution)/shard_map/ppermute | solution.py:19
  145.6 4.8 %collective-permute-start.7 = (f32[34,1,128]{2,0,1:T(8,128)S(1)}, f32[34,1,128]{2,0,1:T(8,128)S(1)}, u32[]{:S(2)}, u32[]{:S(2)}) collective-permute-start(f32[34,1,128]{2,0,1:T(8,128)S(1)} %get-tuple-element.71), channel_id=1, source_target_pairs={{1,0},{2,1},{3,2},{4,3},{5,4},{6,5},{7,6},{8,7},{9,8},{10,9},{11,1... | collective-permute-start | bytes 52232 | tf_op jit(solution)/shard_map/ppermute | solution.py:22
  274.9 16.4 %collective-permute-start.8 = (f32[3,1,16,128]{3,2,1,0:T(8,128)S(1)}, f32[3,1,16,128]{3,2,1,0:T(8,128)S(1)}, u32[]{:S(2)}, u32[]{:S(2)}) collective-permute-start(f32[3,1,16,128]{3,2,1,0:T(8,128)S(1)} %get-tuple-element.48), channel_id=1, source_target_pairs={{0,32},{32,64},{64,96},{96,128},{128,160},{160,192},{192,224},{224... | collective-permute-start | bytes 73736 | tf_op jit(solution)/shard_map/ppermute | solution.py:19
  289.8 4.5 %collective-permute-start.9 = (f32[3,1,16,128]{3,2,1,0:T(8,128)S(1)}, f32[3,1,16,128]{3,2,1,0:T(8,128)S(1)}, u32[]{:S(2)}, u32[]{:S(2)}) collective-permute-start(f32[3,1,16,128]{3,2,1,0:T(8,128)S(1)} %get-tuple-element.49), channel_id=1, source_target_pairs={{32,0},{64,32},{96,64},{128,96},{160,128},{192,160},{224,192},{0,2... | collective-permute-start | bytes 73736 | tf_op jit(solution)/shard_map/ppermute | solution.py:22
  294.4 7.2 %collective-permute-start.10 = (f32[3,34,1,128]{3,2,1,0:T(1,128)S(1)}, f32[3,34,1,128]{3,2,1,0:T(1,128)S(1)}, u32[]{:S(2)}, u32[]{:S(2)}) collective-permute-start(f32[3,34,1,128]{3,2,1,0:T(1,128)S(1)} %get-tuple-element.46), channel_id=1, source_target_pairs={{0,1},{1,2},{2,3},{3,4},{4,5},{5,6},{6,7},{7,8},{8,9},{9,10},{10,1... | collective-permute-start | bytes 156680 | tf_op jit(solution)/shard_map/ppermute | solution.py:19
  295.6 6.0 %collective-permute-start.11 = (f32[3,34,1,128]{3,2,1,0:T(1,128)S(1)}, f32[3,34,1,128]{3,2,1,0:T(1,128)S(1)}, u32[]{:S(2)}, u32[]{:S(2)}) collective-permute-start(f32[3,34,1,128]{3,2,1,0:T(1,128)S(1)} %get-tuple-element.47), channel_id=1, source_target_pairs={{1,0},{2,1},{3,2},{4,3},{5,4},{6,5},{7,6},{8,7},{9,8},{10,9},{11,1... | collective-permute-start | bytes 156680 | tf_op jit(solution)/shard_map/ppermute | solution.py:22
  301.7 1.0 copy-start.11
  301.7 1.0 copy-start.12
  303.2 1.5 collective-permute-start.12
  303.9 4.3 %collective-permute-start.13 = (f32[1,16,128]{2,0,1:T(1,128)S(1)}, f32[1,16,128]{2,0,1:T(1,128)S(1)}, u32[]{:S(2)}, u32[]{:S(2)}) collective-permute-start(f32[1,16,128]{2,0,1:T(1,128)S(1)} %get-tuple-element.75), channel_id=1, source_target_pairs={{32,0},{64,32},{96,64},{128,96},{160,128},{192,160},{224,192},{0,2... | collective-permute-start | bytes 24584 | tf_op jit(solution)/shard_map/ppermute | solution.py:22
  308.2 6.4 %collective-permute-start.14 = (f32[34,1,128]{2,0,1:T(8,128)S(1)}, f32[34,1,128]{2,0,1:T(8,128)S(1)}, u32[]{:S(2)}, u32[]{:S(2)}) collective-permute-start(f32[34,1,128]{2,0,1:T(8,128)S(1)} %get-tuple-element.68), channel_id=1, source_target_pairs={{0,1},{1,2},{2,3},{3,4},{4,5},{5,6},{6,7},{7,8},{8,9},{9,10},{10,1... | collective-permute-start | bytes 52232 | tf_op jit(solution)/shard_map/ppermute | solution.py:19
  308.3 6.4 %collective-permute-start.15 = (f32[34,1,128]{2,0,1:T(8,128)S(1)}, f32[34,1,128]{2,0,1:T(8,128)S(1)}, u32[]{:S(2)}, u32[]{:S(2)}) collective-permute-start(f32[34,1,128]{2,0,1:T(8,128)S(1)} %get-tuple-element.69), channel_id=1, source_target_pairs={{1,0},{2,1},{3,2},{4,3},{5,4},{6,5},{7,6},{8,7},{9,8},{10,9},{11,1... | collective-permute-start | bytes 52232 | tf_op jit(solution)/shard_map/ppermute | solution.py:22
  315.3 1.7 collective-permute-start.16
  316.2 4.3 %collective-permute-start.17 = (f32[1,16,128]{2,0,1:T(1,128)S(1)}, f32[1,16,128]{2,0,1:T(1,128)S(1)}, u32[]{:S(2)}, u32[]{:S(2)}) collective-permute-start(f32[1,16,128]{2,0,1:T(1,128)S(1)} %get-tuple-element.73), channel_id=1, source_target_pairs={{32,0},{64,32},{96,64},{128,96},{160,128},{192,160},{224,192},{0,2... | collective-permute-start | bytes 24584 | tf_op jit(solution)/shard_map/ppermute | solution.py:22
  320.5 6.6 %collective-permute-start.18 = (f32[34,1,128]{2,0,1:T(8,128)S(1)}, f32[34,1,128]{2,0,1:T(8,128)S(1)}, u32[]{:S(2)}, u32[]{:S(2)}) collective-permute-start(f32[34,1,128]{2,0,1:T(8,128)S(1)} %get-tuple-element.66), channel_id=1, source_target_pairs={{0,1},{1,2},{2,3},{3,4},{4,5},{5,6},{6,7},{7,8},{8,9},{9,10},{10,1... | collective-permute-start | bytes 52232 | tf_op jit(solution)/shard_map/ppermute | solution.py:19
  320.6 6.5 %collective-permute-start.19 = (f32[34,1,128]{2,0,1:T(8,128)S(1)}, f32[34,1,128]{2,0,1:T(8,128)S(1)}, u32[]{:S(2)}, u32[]{:S(2)}) collective-permute-start(f32[34,1,128]{2,0,1:T(8,128)S(1)} %get-tuple-element.67), channel_id=1, source_target_pairs={{1,0},{2,1},{3,2},{4,3},{5,4},{6,5},{7,6},{8,7},{9,8},{10,9},{11,1... | collective-permute-start | bytes 52232 | tf_op jit(solution)/shard_map/ppermute | solution.py:22
  328.8 1.2 copy-start.1
